TPU v7x, 512 devices: a whole 4x4x16 slice. The times are simulated.
512 devices in a mesh: ctx: 16 (over z), head: 32 (over x, y, core).
Axes of the slice: x: 4, y: 4, z: 16, core: 2. Of those that a mesh axis runs over, the one named last changes fastest.
Arguments:
- tokens_in: bfloat16 [4096, 4096], P('ctx', 'head'), may hold values from -6 to 6
- w_qkv: bfloat16 [4096, 32, 384], P(None, 'head'), may hold values from -0.125 to 0.125
- w_out: bfloat16 [32, 128, 4096], P('head'), may hold values from -0.375 to 0.375
- codebook: bfloat16 [32, 512, 128], P('head'), may hold values from -184 to 184
- codes: int32 [32, 4096], P('head', 'ctx'), may hold values from 0 to 511
- reach: int32 [16], P('ctx'), may hold values from 1 to 256, as said below
Outputs:
- mixed: bfloat16 [4096, 4096], P(('ctx', 'head'))
Inputs may be any that keep to these rules, and one draw needn't show every extreme that they name: reach[g] is how many of the last positions of block g - 1 block g sees with exact keys; reach[0] has no effect.
All inputs are finite; a program needn't handle non-finite values.
Results may differ from a plain program's by a relative error of at most 0.015.
Values may be sent and summed in bfloat16 or wider, within the bound.
No kernel may reach another device: no remote copies, remote signals or barrier semaphores. Data moves between devices by JAX's collectives and lax.ppermute only.
A program may use at most 64 MiB of HBM per device.

v0:
```python
import math
import jax
import jax.numpy as jnp
from jax import lax
from jax.sharding import PartitionSpec as P

BLK = 256


def from_behind(block, axis, distance):
    devices = range(lax.axis_size(axis))
    route = [(i - distance, i) for i in devices if i - distance in devices]
    return lax.ppermute(block, axis, route)


def entering(value, axis, combine, identity):
    devices, index = (lax.axis_size(axis), lax.axis_index(axis))
    everything = jax.tree.map(
        lambda part, kind: lax.all_gather(part.astype(kind), axis),
        value,
        (jnp.bfloat16, jnp.bfloat16),
    )
    start = jax.tree.map(
        lambda part, zero: jnp.broadcast_to(jnp.asarray(zero, part.dtype), part.shape),
        value,
        identity,
    )

    def turn(k, before):
        reached = k < index
        new = combine(
            before, jax.tree.map(lambda part, own: part[k].astype(own.dtype), everything, value)
        )
        return jax.tree.map(lambda a, b: jnp.where(reached, a, b), new, before)

    return lax.fori_loop(0, devices, turn, start)


def attend_block(
    queries, keys_win, vals_win, cache_v, cache_c, book, reach_one, prev_flag, block_len, scale
):
    exact = (
        lax.dot_general(
            queries, keys_win, (((1,), (1,)), ((), ())), preferred_element_type=jnp.float32
        )
        * scale
    )
    coded = (
        lax.dot_general(queries, book, (((1,), (1,)), ((), ())), preferred_element_type=jnp.float32)
        * scale
    )
    rows = lax.broadcasted_iota(jnp.int32, exact.shape, 0)
    cols = lax.broadcasted_iota(jnp.int32, exact.shape, 1)
    prev_ok = (cols < block_len) & (cols >= block_len - reach_one) & prev_flag
    curr_ok = (cols >= block_len) & (cols - block_len <= rows)
    allowed = prev_ok | curr_ok
    valid = cache_c > 0.5
    top = jnp.maximum(
        jnp.max(jnp.where(allowed, exact, -jnp.inf), axis=1),
        jnp.max(jnp.where(valid[None, :], coded, -jnp.inf), axis=1),
    )
    probs = jnp.exp(jnp.where(allowed, exact - top[:, None], -jnp.inf))
    weights = jnp.exp(jnp.where(valid[None, :], coded - top[:, None], -jnp.inf))
    numer = jnp.dot(probs.astype(jnp.bfloat16), vals_win, preferred_element_type=jnp.float32)
    numer = numer + jnp.dot(weights, cache_v, precision=lax.Precision.HIGHEST)
    denom = jnp.sum(probs, axis=1) + jnp.dot(weights, cache_c, precision=lax.Precision.HIGHEST)
    return (numer / denom[:, None]).astype(jnp.bfloat16)


def combine(earlier, later):
    return (earlier[0] + later[0], earlier[1] + later[1])


def on_device(tokens_in, w_qkv, w_out, codebook, codes, reach):
    tok_rows = tokens_in.shape[0]
    head_dim = codebook.shape[2]
    num_codes = codebook.shape[1]
    num_blocks = tok_rows // BLK
    scale = 1.0 / math.sqrt(head_dim)
    w_local = w_qkv[:, 0, :]
    projected = jnp.dot(
        lax.all_gather(tokens_in, "head", axis=1, tiled=True),
        w_local,
        preferred_element_type=jnp.float32,
    )
    queries = projected[:, :head_dim].astype(jnp.bfloat16)
    key_vals = projected[:, head_dim:].astype(jnp.bfloat16)
    code_row = codes[0]
    book = codebook[0]
    prev_kv, prev_codes = from_behind((key_vals, code_row), "ctx", 1)
    has_prev = lax.axis_index("ctx") > 0
    code_ids = jnp.arange(num_codes, dtype=jnp.int32)
    onehot_loc = (code_row[:, None] == code_ids[None, :]).astype(jnp.bfloat16)
    local_v = jnp.einsum(
        "ts,td->sd", onehot_loc, key_vals[:, head_dim:], preferred_element_type=jnp.float32
    )
    local_c = jnp.sum(onehot_loc, axis=0, dtype=jnp.float32)
    before_v, before_c = entering(
        (local_v, local_c), "ctx", combine, (jnp.zeros_like(local_v), jnp.zeros_like(local_c))
    )
    ext_kv = jnp.concatenate([prev_kv, key_vals], axis=0)
    ext_codes = jnp.concatenate([prev_codes, code_row], axis=0)
    ext_len = BLK + tok_rows
    positions = jnp.arange(ext_len, dtype=jnp.int32)[:, None]
    thresholds = (jnp.arange(num_blocks, dtype=jnp.int32) + 1) * BLK - reach
    plus = (positions >= BLK) & (positions < thresholds[None, :])
    minus = (positions < BLK) & (positions >= thresholds[None, :]) & has_prev
    signs = (plus.astype(jnp.float32) - minus.astype(jnp.float32)).astype(jnp.bfloat16)
    signed_vals = (signs[:, :, None] * ext_kv[:, None, head_dim:]).reshape(
        ext_len, num_blocks * head_dim
    )
    onehot_ext = (ext_codes[:, None] == code_ids[None, :]).astype(jnp.bfloat16)
    part_v = jnp.einsum(
        "es,ef->sf", onehot_ext, signed_vals, preferred_element_type=jnp.float32
    ).reshape(num_codes, num_blocks, head_dim)
    part_c = jnp.einsum("es,eb->sb", onehot_ext, signs, preferred_element_type=jnp.float32)
    cache_v = before_v + part_v[:, 0, :]
    cache_c = before_c + part_c[:, 0]
    prev_flag = has_prev | (0 > 0)
    pieces_out = attend_block(
        queries,
        ext_kv[:, :head_dim],
        ext_kv[:, head_dim:],
        cache_v,
        cache_c,
        book,
        reach[0],
        prev_flag,
        BLK,
        scale,
    )
    w_proj = w_out[0]
    mixed = lax.psum_scatter(
        jnp.dot(pieces_out, w_proj, preferred_element_type=jnp.float32).astype(jnp.bfloat16),
        "head",
        scatter_dimension=0,
        tiled=True,
    )
    return mixed


def solution(mesh):
    in_specs = (
        P("ctx", "head"),
        P(None, "head", None),
        P("head", None, None),
        P("head", None, None),
        P("head", "ctx"),
        P("ctx"),
    )
    out_specs = P(("ctx", "head"), None)
    return jax.shard_map(
        on_device, mesh=mesh, in_specs=in_specs, out_specs=out_specs, check_vma=False
    )
```

profile of v0, /device:TPU:2, one launch (start us, length us, event | category | flops | bytes accessed | tf_op | source)
XLA Modules:
  0.0 296.4 jit_solution(15039246053632858118)
XLA Ops:
  7.3 67.3 %all-gather.6.cloned.1.call-done = bf16[256,4096]{1,0:T(8,128)(2,1)} async-done(((bf16[256,128]{1,0:T(8,128)(2,1)}), bf16[256,4096]{1,0:T(8,128)(2,1)}) %all-gather.6.cloned.1.call-update) | async-done | bytes 2097168 | tf_op jit(solution)/shard_map/all_gather | solution.py:82
  74.7 2.8 fusion.2
  78.2 1.1 convolution_convert_fusion.1
  79.3 3.5 %collective-permute-start.1 = (s32[256]{0:T(256)S(1)}, s32[256]{0:T(256)S(1)}, u32[]{:S(2)}, u32[]{:S(2)}) collective-permute-start(s32[256]{0:T(256)S(1)} %bitcast.40), channel_id=1, source_target_pairs={{0,32},{32,64},{64,96},{96,128},{128,160},{160,192},{192,224},{224... | collective-permute-start | bytes 3080 | tf_op jit(solution)/shard_map/ppermute | solution.py:13
  83.7 29.7 %all-gather.2 = bf16[16,1,512]{2,1,0:T(2,128)(2,1)S(1)} all-gather(bf16[1,1,512]{2,1,0:T(2,128)(2,1)S(1)} %reshape.63), channel_id=3, replica_groups=mesh['ctx'=16,'head'=32] {'ctx'}, dimensions={0}, use_global_device_ids=true | all-gather | bytes 17408 | tf_op jit(solution)/shard_map/all_gather | solution.py:19
  114.9 1.8 collective-permute-start
  117.7 2.1 collective-permute-done
  120.5 2.5 select_reduce_fusion.1
  122.9 29.8 %all-gather.8.cloned.1.call-done = bf16[8192,128]{1,0:T(8,128)(2,1)} async-done(((bf16[512,128]{1,0:T(8,128)(2,1)}), bf16[8192,128]{1,0:T(8,128)(2,1)}) %all-gather.8.cloned.1.call-update) | async-done | bytes 2097168 | tf_op jit(solution)/shard_map/all_gather | solution.py:19
  152.8 28.5 %while.16 = (s32[]{:T(128)}, f32[512,128]{1,0:T(8,128)S(1)}, f32[512]{0:T(512)S(1)}, s32[]{:T(128)}, bf16[16,512,128]{2,1,0:T(8,128)(2,1)}, /*index=5*/bf16[16,512]{1,0:T(8,128)(2,1)}, s32[]{:T(128)}, s32[]{:T(128)}) while((s32[]{:T(128)}, f32[512,128]{1,0:T(8,128)S(1)}, f32[512]{0:T(512)S(1)}, s32[]{:T(128)}, ...), condition=%wide.region_3.4_spmd.clone, body=%wide.region_2.3_spmd.clone.sunk | while | flops 264196 | bytes 664699 | solution.py:36
  154.5 1.0 add_select_fusion.4
  156.3 1.0 add_select_fusion.4
  158.1 1.0 add_select_fusion.4
  159.9 1.0 add_select_fusion.4
  161.7 1.0 add_select_fusion.4
  163.4 1.0 add_select_fusion.4
  165.2 1.0 add_select_fusion.4
  167.0 1.0 add_select_fusion.4
  168.8 1.0 add_select_fusion.4
  181.9 1.3 select_reduce_fusion
  183.8 1.3 fusion.16
  185.1 1.5 convolution_add_fusion
  187.9 3.7 %convolution_convert_fusion = bf16[256,4096]{1,0:T(8,128)(2,1)} fusion(f32[256,128]{1,0:T(8,128)S(1)} %fusion.15, bf16[1,128,4096]{2,1,0:T(8,128)(2,1)} %param.10, f32[256,512]{1,0:T(8,128)} %get-tuple-element.153, f32[256]{0:T(256)S(1)} %max.7, s32[512]{0:T(512)S(1)} %iota_add_fusion, pred[512]{0:T(512)(128)(4,1)S(1)} %get-tuple-element.156, ...), kind=kOutput, calls=%fused_computation.3 | convolution fusion | flops 304185344 | bytes 4068352 | tf_op jit(solution)/shard_map/dot_general | solution.py:134
  191.7 98.2 %reduce-scatter.2.cloned.1.call-done = bf16[8,4096]{1,0:T(8,128)(2,1)} async-done(((bf16[256,4096]{1,0:T(8,128)(2,1)}), bf16[8,4096]{1,0:T(8,128)(2,1)}) %reduce-scatter.2.cloned.1.call-update) | async-done | bytes 65552 | tf_op jit(solution)/shard_map/reduce_scatter | solution.py:133
  (75 shorter events, 26.2 us)
Async XLA Ops:
  6.5 68.1 %copy-start = (bf16[4096,1,384]{2,0,1:T(8,128)(2,1)S(1)}, bf16[4096,1,384]{2,0,1:T(8,128)(2,1)}, u32[]{:S(2)}) copy-start(bf16[4096,1,384]{2,0,1:T(8,128)(2,1)} %param.9) | copy-start | bytes 9437188
  6.5 68.1 %all-gather.6.cloned.1.call-start = ((), (), s32[]{:S(2)}) async-start(), calls=%async_computation.1 | async-start | bytes 2162688 | tf_op jit(solution)/shard_map/all_gather | solution.py:82
  7.3 70.9 %copy-start.4 = (s32[1,256]{1,0:T(1,128)S(1)}, s32[1,256]{1,0:T(1,128)}, u32[]{:S(2)}) copy-start(s32[1,256]{1,0:T(1,128)} %param.12) | copy-start | bytes 3076
  7.3 145.5 %all-gather.8.cloned.1.call-start = ((), (), s32[]{:S(2)}) async-start(), calls=%async_computation.3 | async-start | bytes 2228224 | tf_op jit(solution)/shard_map/all_gather | solution.py:19
  77.5 0.7 copy-start.1
  79.3 210.6 %reduce-scatter.2.cloned.1.call-start = ((), (), s32[]{:S(2)}) async-start(), calls=%async_computation.2 | async-start | bytes 2162688 | tf_op jit(solution)/shard_map/reduce_scatter | solution.py:133
  79.3 34.6 %collective-permute-start.1 = (s32[256]{0:T(256)S(1)}, s32[256]{0:T(256)S(1)}, u32[]{:S(2)}, u32[]{:S(2)}) collective-permute-start(s32[256]{0:T(256)S(1)} %bitcast.40), channel_id=1, source_target_pairs={{0,32},{32,64},{64,96},{96,128},{128,160},{160,192},{192,224},{224... | collective-permute-start | bytes 3080 | tf_op jit(solution)/shard_map/ppermute | solution.py:13
  83.6 30.3 %copy-start.3 = (bf16[512]{0:T(512)(128)(2,1)}, bf16[512]{0:T(512)(128)(2,1)S(1)}, u32[]{:S(2)}) copy-start(bf16[512]{0:T(512)(128)(2,1)S(1)} %subtract_convert_fusion) | copy-start | bytes 3076
  114.0 5.8 %copy-start.5 = (s32[512]{0:T(512)}, s32[512]{0:T(512)S(1)}, u32[]{:S(2)}) copy-start(s32[512]{0:T(512)S(1)} %pad_add_fusion) | copy-start | bytes 6148
  114.9 4.9 %collective-permute-start = (bf16[256,256]{1,0:T(8,128)(2,1)S(1)}, bf16[256,256]{1,0:T(8,128)(2,1)S(1)}, u32[]{:S(2)}, u32[]{:S(2)}) collective-permute-start(bf16[256,256]{1,0:T(8,128)(2,1)S(1)} %slice.25), channel_id=1, source_target_pairs={{0,32},{32,64},{64,96},{96,128},{128,160},{160,192},{192,224},{224... | collective-permute-start | bytes 393224 | tf_op jit(solution)/shard_map/ppermute | solution.py:13
  119.8 0.7 copy-start.2
Sparse Core Ops, SparseCore 0:
  10.4 64.1 all-gather.5
  79.4 73.3 all-gather.7
  191.8 98.0 reduce-scatter.1
where the time goes:
time: 298 us; the launch traced here: 296 us
  waiting for transfers between devices  198 us (66%)
  other arithmetic  31 us (10%)
  blocking collectives  29.7 us (10%)
  matrix products  15 us (5%)
  between operations  13.9 us (5%)
  starting transfers between devices  5.39 us (2%)
    reduce_scatter x1, waiting for transfers between devices, on_device(): lax.psum_scatter(jnp.dot(pieces_out, w_proj, preferred_element_type=jnp.f...  98.2 us
    all_gather x1, waiting for transfers between devices, on_device(): lax.all_gather(tokens_in, 'head', axis=1, tiled=True)  67.3 us
    all_gather x1, waiting for transfers between devices, entering(): lax.all_gather(part.astype(kind), axis)  29.8 us
    all_gather x1, blocking collectives, entering(): lax.all_gather(part.astype(kind), axis)  29.7 us
    select_n x32, other arithmetic, turn(): return jax.tree.map(lambda a, b: jnp.where(reached, a, b), new, before)  16.8 us
    convert_element_type x16, other arithmetic, turn(): part[k].astype(own.dtype)  11.3 us
  transfers between devices with their start and end apart: 5, of which 4 were waited for; matrix products, arithmetic and copies ran while one was open for 2% of the time, Pallas kernels for 0%

commit v1 on v0

--- a/solution.py
+++ b/solution.py
@@ -79,7 +79,9 @@
     scale = 1.0 / math.sqrt(head_dim)
     w_local = w_qkv[:, 0, :]
     projected = jnp.dot(
-        lax.all_gather(tokens_in, "head", axis=1, tiled=True),
+        jnp.concatenate(
+            lax.all_to_all(jnp.stack([tokens_in] * lax.axis_size("head")), "head", 0, 0), axis=1
+        ),
         w_local,
         preferred_element_type=jnp.float32,
     )

time: 298 us -> 267 us (0.90)
  waiting for transfers between devices: 198 us -> 129 us
  blocking collectives: 29.7 us -> 67.8 us
    all_gather x1 -> x0, waiting for transfers between devices: 67.3 us -> none  [on_device(): lax.all_gather(tokens_in, 'head', axis=1, tiled=True)]
    all_to_all x0 -> x1, blocking collectives: none -> 34.4 us  [on_device(): lax.all_to_all(jnp.stack([tokens_in] * lax.axis_size('head')), 'head', 0, 0)]
    all_gather x1, blocking collectives: 29.7 us -> 33.5 us  [entering(): lax.all_gather(part.astype(kind), axis)]
  transfers between devices with their start and end apart: 5 -> 4, of which waited for: 4 -> 3; matrix products, arithmetic and copies ran while one was open for 2% -> 2% of each run, Pallas kernels for 0% -> 0%
where the time goes in v1:
time: 267 us; the launch traced here: 265 us
  waiting for transfers between devices  129 us (48%)
  blocking collectives  67.8 us (25%)
  other arithmetic  31 us (12%)
  between operations  14.2 us (5%)
  matrix products  13.5 us (5%)
  starting transfers between devices  5.51 us (2%)
  local copies, waits for them, and re-layouts  4.19 us (2%)
    reduce_scatter x1, waiting for transfers between devices, on_device(): lax.psum_scatter(jnp.dot(pieces_out, w_proj, preferred_element_type=jnp.f...  98.5 us
    all_to_all x1, blocking collectives, on_device(): lax.all_to_all(jnp.stack([tokens_in] * lax.axis_size('head')), 'head', 0, 0)  34.4 us
    all_gather x1, blocking collectives, entering(): lax.all_gather(part.astype(kind), axis)  33.5 us
    all_gather x1, waiting for transfers between devices, entering(): lax.all_gather(part.astype(kind), axis)  27.2 us
    select_n x32, other arithmetic, turn(): return jax.tree.map(lambda a, b: jnp.where(reached, a, b), new, before)  16.8 us
    convert_element_type x16, other arithmetic, turn(): part[k].astype(own.dtype)  11.3 us
    ppermute x2, starting transfers between devices, from_behind(): return lax.ppermute(block, axis, route)  5.46 us
  transfers between devices with their start and end apart: 4, of which 3 were waited for; matrix products, arithmetic and copies ran while one was open for 2% of the time, Pallas kernels for 0%

profile of v1, /device:TPU:2, one launch (start us, length us, event | category | flops | bytes accessed | tf_op | source)
XLA Modules:
  0.0 265.4 jit_solution(12854401037894120917)
XLA Ops:
  6.5 1.1 copy.10
  7.9 34.4 %all_to_all.5 = bf16[32,256,128]{1,2,0:T(8,128)(2,1)S(1)} all-to-all(bf16[32,256,128]{1,2,0:T(8,128)(2,1)S(1)} %stack.2), channel_id=1, replica_groups=mesh['ctx'=16,'head'=32] {'head'}, dimensions={0} | all-to-all | bytes 4194304 | tf_op jit(solution)/shard_map/all_to_all | solution.py:83
  42.2 1.3 fusion.2
  44.2 1.1 convolution_convert_fusion.1
  45.4 2.5 collective-permute-start.1
  48.8 33.5 %all-gather.2 = bf16[16,1,512]{2,1,0:T(2,128)(2,1)S(1)} all-gather(bf16[1,1,512]{2,1,0:T(2,128)(2,1)S(1)} %reshape.73), channel_id=3, replica_groups=mesh['ctx'=16,'head'=32] {'ctx'}, dimensions={0}, use_global_device_ids=true | all-gather | bytes 17408 | tf_op jit(solution)/shard_map/all_gather | solution.py:19
  83.8 2.9 %collective-permute-start = (bf16[256,256]{1,0:T(8,128)(2,1)S(1)}, bf16[256,256]{1,0:T(8,128)(2,1)S(1)}, u32[]{:S(2)}, u32[]{:S(2)}) collective-permute-start(bf16[256,256]{1,0:T(8,128)(2,1)S(1)} %slice.25), channel_id=1, source_target_pairs={{0,32},{32,64},{64,96},{96,128},{128,160},{160,192},{192,224},{224... | collective-permute-start | bytes 393224 | tf_op jit(solution)/shard_map/ppermute | solution.py:13
  87.7 3.1 %collective-permute-done = bf16[256,256]{1,0:T(8,128)(2,1)S(1)} collective-permute-done((bf16[256,256]{1,0:T(8,128)(2,1)S(1)}, bf16[256,256]{1,0:T(8,128)(2,1)S(1)}, u32[]{:S(2)}, u32[]{:S(2)}) %collective-permute-start) | collective-permute-done | bytes 131104 | tf_op jit(solution)/shard_map/ppermute | solution.py:13
  91.5 2.5 select_reduce_fusion.1
  93.9 27.2 %all-gather.5.cloned.1.call-done = bf16[8192,128]{1,0:T(8,128)(2,1)} async-done(((bf16[512,128]{1,0:T(8,128)(2,1)}), bf16[8192,128]{1,0:T(8,128)(2,1)}) %all-gather.5.cloned.1.call-update) | async-done | bytes 2097168 | tf_op jit(solution)/shard_map/all_gather | solution.py:19
  121.1 28.5 %while.16 = (s32[]{:T(128)}, f32[512,128]{1,0:T(8,128)S(1)}, f32[512]{0:T(512)S(1)}, s32[]{:T(128)}, bf16[16,512,128]{2,1,0:T(8,128)(2,1)}, /*index=5*/bf16[16,512]{1,0:T(8,128)(2,1)}, s32[]{:T(128)}, s32[]{:T(128)}) while((s32[]{:T(128)}, f32[512,128]{1,0:T(8,128)S(1)}, f32[512]{0:T(512)S(1)}, s32[]{:T(128)}, ...), condition=%wide.region_3.4_spmd.clone, body=%wide.region_2.3_spmd.clone.sunk | while | flops 264196 | bytes 664691 | solution.py:36
  122.9 1.0 add_select_fusion.4
  124.7 1.0 add_select_fusion.4
  126.5 1.0 add_select_fusion.4
  128.3 1.0 add_select_fusion.4
  130.0 1.0 add_select_fusion.4
  131.8 1.0 add_select_fusion.4
  133.6 1.0 add_select_fusion.4
  135.4 1.0 add_select_fusion.4
  150.3 1.3 select_reduce_fusion
  152.2 1.3 fusion.16
  154.2 1.5 convolution_add_fusion
  156.3 3.7 %convolution_convert_fusion = bf16[256,4096]{1,0:T(8,128)(2,1)} fusion(f32[256,128]{1,0:T(8,128)S(1)} %fusion.15, bf16[1,128,4096]{2,1,0:T(8,128)(2,1)} %param.10, f32[256,512]{1,0:T(8,128)} %get-tuple-element.153, f32[256]{0:T(256)S(1)} %max.7, s32[512]{0:T(512)S(1)} %iota_add_fusion, pred[512]{0:T(512)(128)(4,1)S(1)} %get-tuple-element.156, ...), kind=kOutput, calls=%fused_computation.3 | convolution fusion | flops 304185344 | bytes 4068352 | tf_op jit(solution)/shard_map/dot_general | solution.py:136
  160.1 98.5 %reduce-scatter.2.cloned.1.call-done = bf16[8,4096]{1,0:T(8,128)(2,1)} async-done(((bf16[256,4096]{1,0:T(8,128)(2,1)}), bf16[8,4096]{1,0:T(8,128)(2,1)}) %reduce-scatter.2.cloned.1.call-update) | async-done | bytes 65552 | tf_op jit(solution)/shard_map/reduce_scatter | solution.py:135
  (75 shorter events, 26.8 us)
Async XLA Ops:
  6.5 35.7 %copy-start = (bf16[4096,1,384]{2,0,1:T(8,128)(2,1)S(1)}, bf16[4096,1,384]{2,0,1:T(8,128)(2,1)}, u32[]{:S(2)}) copy-start(bf16[4096,1,384]{2,0,1:T(8,128)(2,1)} %param.9) | copy-start | bytes 9437188
  6.5 114.6 %all-gather.5.cloned.1.call-start = ((), (), s32[]{:S(2)}) async-start(), calls=%async_computation.3 | async-start | bytes 2228224 | tf_op jit(solution)/shard_map/all_gather | solution.py:19
  42.2 2.0 copy-start.4
  43.5 0.7 copy-start.1
  45.3 213.3 %reduce-scatter.2.cloned.1.call-start = ((), (), s32[]{:S(2)}) async-start(), calls=%async_computation.2 | async-start | bytes 2162688 | tf_op jit(solution)/shard_map/reduce_scatter | solution.py:135
  45.4 37.5 %collective-permute-start.1 = (s32[256]{0:T(256)S(1)}, s32[256]{0:T(256)S(1)}, u32[]{:S(2)}, u32[]{:S(2)}) collective-permute-start(s32[256]{0:T(256)S(1)} %bitcast.44), channel_id=1, source_target_pairs={{0,32},{32,64},{64,96},{96,128},{128,160},{160,192},{192,224},{224... | collective-permute-start | bytes 3080 | tf_op jit(solution)/shard_map/ppermute | solution.py:13
  48.8 34.1 %copy-start.3 = (bf16[512]{0:T(512)(128)(2,1)}, bf16[512]{0:T(512)(128)(2,1)S(1)}, u32[]{:S(2)}) copy-start(bf16[512]{0:T(512)(128)(2,1)S(1)} %subtract_convert_fusion) | copy-start | bytes 3076
  82.9 7.9 %copy-start.5 = (s32[512]{0:T(512)}, s32[512]{0:T(512)S(1)}, u32[]{:S(2)}) copy-start(s32[512]{0:T(512)S(1)} %pad_add_fusion) | copy-start | bytes 6148
  83.8 7.0 %collective-permute-start = (bf16[256,256]{1,0:T(8,128)(2,1)S(1)}, bf16[256,256]{1,0:T(8,128)(2,1)S(1)}, u32[]{:S(2)}, u32[]{:S(2)}) collective-permute-start(bf16[256,256]{1,0:T(8,128)(2,1)S(1)} %slice.25), channel_id=1, source_target_pairs={{0,32},{32,64},{64,96},{96,128},{128,160},{160,192},{192,224},{224... | collective-permute-start | bytes 393224 | tf_op jit(solution)/shard_map/ppermute | solution.py:13
  90.8 0.6 copy-start.2
Sparse Core Ops, SparseCore 0:
  45.5 75.6 all-gather.4
  160.2 98.3 reduce-scatter.1
